TPU v7x, 256 devices: a whole 4x4x8 slice. The times are simulated.
256 devices in a mesh: seq: 32 (over z_lo, y, core), head: 8 (over x, z_hi).
Axes of the slice: x: 4, y: 4, z: 8 (z_hi: 2, z_lo: 4; z = z_hi * 4 + z_lo), core: 2. Of those that a mesh axis runs over, the one named last changes fastest.
Arguments:
- queries: bfloat16 [16384, 1024], P('seq', 'head'), may hold values from -2.5 to 2.5
- keys: bfloat16 [16384, 1024], P('seq', 'head'), may hold values from -2.5 to 2.5
- values: bfloat16 [16384, 1024], P('seq', 'head'), may hold values from -6 to 6
- attn_out: bfloat16 [16384, 1024], P('seq', 'head'), may hold values from -6 to 6
- out_grad: bfloat16 [16384, 1024], P('seq', 'head'), may hold values from -6 to 6
- lse: float32 [8, 16384], P('head', 'seq'), may hold values from 3.5 to 5.5
- trace_id: int32 [16384], replicated, may hold values from 0 to 127, never falling along the last dimension, each value on 1 to 384 neighbouring positions
- key_tiles: int32 [128, 48], P('seq'), may hold values from 0 to 127, as said below
- tile_count: int32 [128], P('seq'), may hold values from 1 to 48, as said below
- w_query: bfloat16 [1024, 1024], P(None, 'head'), may hold values from -0.1875 to 0.1875
- w_key: bfloat16 [1024, 1024], P(None, 'head'), may hold values from -0.1875 to 0.1875
- w_value: bfloat16 [1024, 1024], P(None, 'head'), may hold values from -0.1875 to 0.1875
- w_out: bfloat16 [1024, 1024], P('head'), may hold values from -0.1875 to 0.1875
Outputs:
- d_input: bfloat16 [16384, 1024], P('seq', 'head')
Inputs may be any that keep to these rules, and one draw needn't show every extreme that they name: `key_tiles`: each row lists 48 different key tiles and never its own tile; entries from position tile_count onward are not used. `tile_count`: some query tile uses all 48 entries. `trace_id`: trace numbers never fall along the tokens; one trace spans 384 tokens, none more.
All inputs are finite; a program needn't handle non-finite values.
Results may differ from a plain program's by a relative error of at most 0.015.
Values may be sent and summed in bfloat16 or wider, within the bound.
No kernel may reach another device: no remote copies, remote signals or barrier semaphores. Data moves between devices by JAX's collectives and lax.ppermute only.
A program may use at most 64 MiB of HBM per device.

v0:
```python
import jax
import jax.numpy as jnp
from jax import lax
from jax.sharding import PartitionSpec as P

HD = 128
TILE = 128
SEL = 48


def from_behind(value, axis, by):
    count = lax.axis_size(axis)
    return lax.ppermute(value, axis, [(i, (i + by) % count) for i in range(count)])


def pair_grads(query_heads, key_heads, value_heads, grad_heads, norm_rows, delta_rows, admit):
    scale = query_heads.shape[-1] ** (-0.5)
    scores = (
        jnp.einsum("rhd,chd->hrc", query_heads, key_heads, preferred_element_type=jnp.float32)
        * scale
    )
    probs = jnp.where(admit[None], jnp.exp(scores - norm_rows[:, :, None]), 0.0)
    value_grad = jnp.einsum(
        "hrc,rhd->chd", probs.astype(jnp.bfloat16), grad_heads, preferred_element_type=jnp.float32
    )
    prob_grad = jnp.einsum(
        "rhd,chd->hrc", grad_heads, value_heads, preferred_element_type=jnp.float32
    )
    score_grad = (probs * (prob_grad - delta_rows[:, :, None]) * scale).astype(jnp.bfloat16)
    query_grad = jnp.einsum(
        "hrc,chd->rhd", score_grad, key_heads, preferred_element_type=jnp.float32
    )
    key_grad = jnp.einsum(
        "hrc,rhd->chd", score_grad, query_heads, preferred_element_type=jnp.float32
    )
    return (query_grad, key_grad, value_grad)


def query_grads(query_heads, key_heads, value_heads, grad_heads, norm_rows, delta_rows, admit):
    scale = query_heads.shape[-1] ** (-0.5)
    scores = (
        jnp.einsum("rhd,chd->hrc", query_heads, key_heads, preferred_element_type=jnp.float32)
        * scale
    )
    probs = jnp.where(admit[None], jnp.exp(scores - norm_rows[:, :, None]), 0.0)
    prob_grad = jnp.einsum(
        "rhd,chd->hrc", grad_heads, value_heads, preferred_element_type=jnp.float32
    )
    score_grad = (probs * (prob_grad - delta_rows[:, :, None]) * scale).astype(jnp.bfloat16)
    return jnp.einsum("hrc,chd->rhd", score_grad, key_heads, preferred_element_type=jnp.float32)


def key_grads(query_heads, key_heads, value_heads, grad_heads, norm_cols, delta_cols, admit):
    scale = query_heads.shape[-1] ** (-0.5)
    scores = (
        jnp.einsum("chd,rhd->hcr", key_heads, query_heads, preferred_element_type=jnp.float32)
        * scale
    )
    probs = jnp.where(admit[None], jnp.exp(scores - norm_cols[:, None, :]), 0.0)
    value_grad = jnp.einsum(
        "hcr,rhd->chd", probs.astype(jnp.bfloat16), grad_heads, preferred_element_type=jnp.float32
    )
    prob_grad = jnp.einsum(
        "chd,rhd->hcr", value_heads, grad_heads, preferred_element_type=jnp.float32
    )
    score_grad = (probs * (prob_grad - delta_cols[:, None, :]) * scale).astype(jnp.bfloat16)
    key_grad = jnp.einsum(
        "hcr,rhd->chd", score_grad, query_heads, preferred_element_type=jnp.float32
    )
    return (key_grad, value_grad)


def settle(total):
    part = lax.optimization_barrier(total.astype(jnp.bfloat16))
    return part.astype(jnp.float32)


def per_device(
    queries,
    keys,
    values,
    attn_out,
    out_grad,
    lse,
    trace_id,
    key_tiles,
    tile_count,
    w_query,
    w_key,
    w_value,
    w_out,
):
    tokens_here, width = queries.shape
    heads_here = width // HD
    seq_count = lax.axis_size("seq")
    seq_index = lax.axis_index("seq")
    tiles_here = tokens_here // TILE
    head_count = lax.axis_size("head")
    head_index = lax.axis_index("head")
    grad_blocks = [out_grad] + [from_behind(out_grad, "head", shift) for shift in range(1, head_count)]
    block_order = (head_index - jnp.arange(head_count)) % head_count
    block_width = out_grad.shape[1]
    w_out_blocks = jnp.take(
        w_out.reshape(w_out.shape[0], head_count, block_width), block_order, axis=1
    ).reshape(w_out.shape[0], head_count * block_width)
    d_attn = lax.dot_general(
        jnp.concatenate(grad_blocks, axis=1),
        w_out_blocks,
        (((1,), (1,)), ((), ())),
        preferred_element_type=jnp.float32,
    ).astype(jnp.bfloat16)
    product = d_attn.astype(jnp.float32) * attn_out.astype(jnp.float32)
    delta = jnp.sum(product.reshape(tokens_here, heads_here, HD), axis=2).T
    query_heads = queries.reshape(tokens_here, heads_here, HD)
    key_heads = keys.reshape(tokens_here, heads_here, HD)
    value_heads = values.reshape(tokens_here, heads_here, HD)
    grad_heads = d_attn.reshape(tokens_here, heads_here, HD)
    trace_here = lax.dynamic_slice_in_dim(trace_id, seq_index * tokens_here, tokens_here, 0)
    slots = jnp.arange(SEL)[None, :] < tile_count[:, None]
    tile_range = jnp.arange(seq_count * tiles_here)
    allowed = jnp.any(
        (key_tiles[:, :, None] == tile_range[None, None, :]) & slots[:, :, None], axis=1
    )

    kv_all = lax.all_gather(jnp.stack([key_heads, value_heads]), "seq", axis=1, tiled=True)
    qg_all = lax.all_gather(jnp.stack([query_heads, grad_heads]), "seq", axis=1, tiled=True)
    grad_all = qg_all[1]
    stats = jnp.concatenate(
        [lse, delta, allowed.astype(jnp.float32).reshape(-1, tokens_here)], axis=0
    )
    stats_all = lax.all_gather(stats, "seq", axis=1, tiled=True)
    total_tokens = kv_all.shape[1]
    lse_all = stats_all[:heads_here]
    delta_all = stats_all[heads_here:2 * heads_here]
    allowed_all = stats_all[2 * heads_here:].reshape(seq_count, tiles_here, -1)
    allowed_all = allowed_all.reshape(seq_count * tiles_here, -1)[:, : seq_count * tiles_here] > 0.5
    chunk = min(total_tokens, 4096)
    query_sum = None
    for first in range(0, total_tokens, chunk):
        listed = allowed[:, first // TILE:(first + chunk) // TILE]
        admit = jnp.repeat(jnp.repeat(listed, TILE, axis=0), TILE, axis=1) & (
            trace_here[:, None] != trace_id[None, first:first + chunk]
        )
        query_add = query_grads(
            query_heads, kv_all[0, first:first + chunk], kv_all[1, first:first + chunk],
            grad_heads, lse, delta, admit,
        )
        query_sum = query_add if query_sum is None else query_sum + query_add
    key_sum = None
    mine = seq_index * tiles_here
    chunk = min(total_tokens, 8192)
    for first in range(0, total_tokens, chunk):
        listed = lax.dynamic_slice_in_dim(allowed_all[first // TILE:(first + chunk) // TILE], mine, tiles_here, 1)
        admit = jnp.repeat(jnp.repeat(listed.T, TILE, axis=0), TILE, axis=1) & (
            trace_here[:, None] != trace_id[None, first:first + chunk]
        )
        key_add, value_add = key_grads(
            qg_all[0, first:first + chunk], key_heads, value_heads, grad_all[first:first + chunk],
            lse_all[:, first:first + chunk], delta_all[:, first:first + chunk], admit,
        )
        if key_sum is None:
            key_sum, value_sum = key_add, value_add
        else:
            key_sum, value_sum = key_sum + key_add, value_sum + value_add
    d_query = query_sum.astype(jnp.bfloat16).reshape(tokens_here, width)
    d_key = key_sum.astype(jnp.bfloat16).reshape(tokens_here, width)
    d_value = value_sum.astype(jnp.bfloat16).reshape(tokens_here, width)
    contract = (((1,), (1,)), ((), ()))
    total = lax.dot_general(w_query, d_query, contract, preferred_element_type=jnp.float32)
    total = total + lax.dot_general(w_key, d_key, contract, preferred_element_type=jnp.float32)
    total = total + lax.dot_general(w_value, d_value, contract, preferred_element_type=jnp.float32)
    total = total.reshape((head_count, total.shape[0] // head_count) + total.shape[1:])
    total = total.astype(jnp.bfloat16)
    d_input = lax.dynamic_index_in_dim(total, head_index, 0, keepdims=False).astype(jnp.float32)
    for shift in range(1, head_count):
        owed = lax.dynamic_index_in_dim(total, (head_index + shift) % head_count, 0, keepdims=False)
        d_input = d_input + from_behind(owed, "head", shift).astype(jnp.float32)
    return d_input.T.astype(jnp.bfloat16)


def solution(mesh):
    in_specs = (
        P("seq", "head"),
        P("seq", "head"),
        P("seq", "head"),
        P("seq", "head"),
        P("seq", "head"),
        P("head", "seq"),
        P(),
        P("seq", None),
        P("seq"),
        P(None, "head"),
        P(None, "head"),
        P(None, "head"),
        P("head", None),
    )
    out_specs = P("seq", "head")
    return jax.shard_map(
        per_device, mesh=mesh, in_specs=in_specs, out_specs=out_specs, check_vma=False
    )
```

profile of v0, /device:TPU:32, one launch (start us, length us, event | category | flops | bytes accessed | tf_op | source)
XLA Modules:
  0.0 279.2 jit_solution(1964148868601232518)
XLA Ops:
  6.6 1.8 pad_maximum_fusion
  8.5 2.8 %collective-permute-start.5 = (bf16[512,128]{1,0:T(8,128)(2,1)}, bf16[512,128]{1,0:T(8,128)(2,1)S(1)}, u32[]{:S(2)}, u32[]{:S(2)}) collective-permute-start(bf16[512,128]{1,0:T(8,128)(2,1)} %param.17), channel_id=1, source_target_pairs={{0,6},{1,7},{2,0},{3,1},{4,2},{5,3},{6,4},{7,5},{8,14},{9,15},{10,... | collective-permute-start | bytes 393224 | tf_op jit(solution)/shard_map/ppermute | solution.py:13
  11.3 6.5 %collective-permute-start.4 = (bf16[512,128]{1,0:T(8,128)(2,1)}, bf16[512,128]{1,0:T(8,128)(2,1)S(1)}, u32[]{:S(2)}, u32[]{:S(2)}) collective-permute-start(bf16[512,128]{1,0:T(8,128)(2,1)} %param.17), channel_id=1, source_target_pairs={{0,5},{1,6},{2,7},{3,0},{4,1},{5,2},{6,3},{7,4},{8,13},{9,14},{10,... | collective-permute-start | bytes 393224 | tf_op jit(solution)/shard_map/ppermute | solution.py:13
  17.8 2.7 collective-permute-start.3
  26.0 10.3 %collective-permute-done = bf16[512,128]{1,0:T(8,128)(2,1)S(1)} collective-permute-done((bf16[512,128]{1,0:T(8,128)(2,1)}, bf16[512,128]{1,0:T(8,128)(2,1)S(1)}, u32[]{:S(2)}, u32[]{:S(2)}) %collective-permute-start) | collective-permute-done | bytes 131104 | tf_op jit(solution)/shard_map/ppermute | solution.py:13
  36.3 3.4 %collective-permute-start.2 = (bf16[512,128]{1,0:T(8,128)(2,1)}, bf16[512,128]{1,0:T(8,128)(2,1)S(1)}, u32[]{:S(2)}, u32[]{:S(2)}) collective-permute-start(bf16[512,128]{1,0:T(8,128)(2,1)} %param.17), channel_id=1, source_target_pairs={{0,3},{1,4},{2,5},{3,6},{4,7},{5,0},{6,1},{7,2},{8,11},{9,12},{10,... | collective-permute-start | bytes 393224 | tf_op jit(solution)/shard_map/ppermute | solution.py:13
  39.8 3.4 %collective-permute-start.6 = (bf16[512,128]{1,0:T(8,128)(2,1)}, bf16[512,128]{1,0:T(8,128)(2,1)S(1)}, u32[]{:S(2)}, u32[]{:S(2)}) collective-permute-start(bf16[512,128]{1,0:T(8,128)(2,1)} %param.17), channel_id=1, source_target_pairs={{0,7},{1,0},{2,1},{3,2},{4,3},{5,4},{6,5},{7,6},{8,15},{9,8},{10,9... | collective-permute-start | bytes 393224 | tf_op jit(solution)/shard_map/ppermute | solution.py:13
  43.2 11.1 %collective-permute-done.2 = bf16[512,128]{1,0:T(8,128)(2,1)S(1)} collective-permute-done((bf16[512,128]{1,0:T(8,128)(2,1)}, bf16[512,128]{1,0:T(8,128)(2,1)S(1)}, u32[]{:S(2)}, u32[]{:S(2)}) %collective-permute-start.2) | collective-permute-done | bytes 131104 | tf_op jit(solution)/shard_map/ppermute | solution.py:13
  54.5 3.0 %collective-permute-done.6 = bf16[512,128]{1,0:T(8,128)(2,1)S(1)} collective-permute-done((bf16[512,128]{1,0:T(8,128)(2,1)}, bf16[512,128]{1,0:T(8,128)(2,1)S(1)}, u32[]{:S(2)}, u32[]{:S(2)}) %collective-permute-start.6) | collective-permute-done | bytes 131104 | tf_op jit(solution)/shard_map/ppermute | solution.py:13
  60.3 37.2 %all_gather.11 = f32[3,16384]{1,0:T(4,128)S(1)} all-gather(f32[3,512]{1,0:T(4,128)S(1)} %pad_maximum_fusion.2), channel_id=1, replica_groups=mesh['seq'=32,'head'=8] {'seq'}, dimensions={1}, use_global_device_ids=true | all-gather | bytes 202752 | tf_op jit(solution)/shard_map/all_gather | solution.py:131
  98.4 2.6 fusion.44
  102.1 5.2 %fusion.6 = bf16[512,4096]{0,1:T(8,128)(2,1)} fusion(f32[4096,512]{1,0:T(8,128)S(1)} %fusion.44, bf16[512,128]{0,1:T(8,128)(2,1)S(1)} %get-tuple-element.29, f32[512]{0:T(512)S(1)} %get-tuple-element.28, f32[512]{0:T(512)S(1)} %bitcast.301, s32[512]{0:T(512)S(1)} %dynamic_slice.34, s32[4096]{0:T(1024)S(1)} %get-tuple-element.20, ...), kind=kOutput, calls=%fused_computation.14 | convolution fusion | flops 555745280 | bytes 13801472 | tf_op jit(solution)/shard_map/rhd,chd->hrc/dot_general | solution.py:46
  108.6 4.0 %fusion.9 = bf16[512,4096]{0,1:T(8,128)(2,1)S(1)} fusion(f32[4096,512]{1,0:T(8,128)S(1)} %fusion.43, bf16[512,128]{0,1:T(8,128)(2,1)S(1)} %get-tuple-element.29, f32[512]{0:T(512)S(1)} %get-tuple-element.28, f32[512]{0:T(512)S(1)} %bitcast.302, s32[512]{0:T(512)S(1)} %dynamic_slice.34, s32[4096]{0:T(1024)S(1)} %get-tuple-element.21, ...), kind=kOutput, calls=%fused_computation.18 | convolution fusion | flops 555745280 | bytes 13801472 | tf_op jit(solution)/shard_map/rhd,chd->hrc/dot_general | solution.py:46
  113.8 4.0 %fusion.12 = bf16[512,4096]{0,1:T(8,128)(2,1)S(1)} fusion(f32[4096,512]{1,0:T(8,128)S(1)} %fusion.42, bf16[512,128]{0,1:T(8,128)(2,1)S(1)} %get-tuple-element.29, f32[512]{0:T(512)S(1)} %get-tuple-element.28, f32[512]{0:T(512)S(1)} %bitcast.303, s32[512]{0:T(512)S(1)} %dynamic_slice.34, s32[4096]{0:T(1024)S(1)} %get-tuple-element.22, ...), kind=kOutput, calls=%fused_computation.22 | convolution fusion | flops 555745280 | bytes 13801472 | tf_op jit(solution)/shard_map/rhd,chd->hrc/dot_general | solution.py:46
  119.0 4.0 %fusion.15 = bf16[512,4096]{0,1:T(8,128)(2,1)S(1)} fusion(f32[4096,512]{1,0:T(8,128)S(1)} %fusion.41, bf16[512,128]{0,1:T(8,128)(2,1)S(1)} %get-tuple-element.29, f32[512]{0:T(512)S(1)} %get-tuple-element.28, f32[512]{0:T(512)S(1)} %bitcast.304, s32[512]{0:T(512)S(1)} %dynamic_slice.34, s32[4096]{0:T(1024)S(1)} %get-tuple-element.23, ...), kind=kOutput, calls=%fused_computation.26 | convolution fusion | flops 555745280 | bytes 13801472 | tf_op jit(solution)/shard_map/rhd,chd->hrc/dot_general | solution.py:46
  125.3 5.1 %fusion.33 = f32[512,1024]{1,0:T(8,128)} fusion(bf16[1024,128]{1,0:T(8,128)(2,1)S(1)} %copy-done, f32[128,512]{1,0:T(8,128)S(1)} %convolution_add_fusion.1, bf16[512,4096]{0,1:T(8,128)(2,1)} %fusion.6, bf16[2,16384,1,128]{3,1,2,0:T(8,128)(2,1)} %all-gather.3.cloned.1.call-done), kind=kOutput, calls=%fused_computation.53 | convolution fusion | flops 671219712 | bytes 7864320 | tf_op jit(solution)/shard_map/dot_general | solution.py:169
  130.4 33.6 %all-gather.5.cloned.1.call-done = bf16[2,16384,1,128]{1,3,2,0:T(8,128)(2,1)} async-done(((bf16[2,512,1,128]{1,3,2,0:T(8,128)(2,1)}), bf16[2,16384,1,128]{1,3,2,0:T(8,128)(2,1)}) %all-gather.5.cloned.1.call-update) | async-done | bytes 8388624 | tf_op jit(solution)/shard_map/all_gather | solution.py:126
  164.1 23.1 %bitcast_select_fusion.1 = f32[512,8192]{0,1:T(8,128)} fusion(bf16[512,128]{1,0:T(8,128)(2,1)S(1)} %copy-done.4, f32[8192]{0:T(1024)S(1)} %bitcast.289, s32[512]{0:T(512)S(1)} %dynamic_slice.34, s32[8192]{0:T(1024)S(1)} %get-tuple-element.19, pred[512,64]{0,1:T(8,128)(4,1)S(1)} %bitcast.285, bf16[2,16384,1,128]{1,3,2,0:T(8,128)(2,1)} %all-gather.5.cloned.1.call-done), kind=kOutput, calls=%fused_computation.8 | convolution fusion | flops 1094713344 | bytes 19105792 | tf_op jit(solution)/shard_map/chd,rhd->hcr/dot_general | solution.py:56
  187.2 11.6 %fusion.20 = f32[128,512]{1,0:T(8,128)S(1)} fusion(f32[512,8192]{0,1:T(8,128)} %bitcast_select_fusion.1, bf16[512,128]{1,0:T(8,128)(2,1)S(1)} %copy-done.5, f32[8192]{0:T(1024)S(1)} %bitcast.288, bf16[2,16384,1,128]{1,3,2,0:T(8,128)(2,1)} %all-gather.5.cloned.1.call-done), kind=kOutput, calls=%fused_computation.35 | convolution fusion | flops 2164260864 | bytes 21397504 | tf_op jit(solution)/shard_map/hcr,rhd->chd/dot_general | solution.py:67
  198.8 10.1 %bitcast_select_fusion = f32[512,8192]{0,1:T(8,128)} fusion(bf16[512,128]{1,0:T(8,128)(2,1)S(1)} %copy-done.4, f32[8192]{0:T(1024)S(1)} %bitcast.287, s32[512]{0:T(512)S(1)} %dynamic_slice.34, s32[8192]{0:T(1024)S(1)} %get-tuple-element.18, pred[512,64]{0,1:T(8,128)(4,1)S(1)} %bitcast.284, bf16[2,16384,1,128]{1,3,2,0:T(8,128)(2,1)} %all-gather.5.cloned.1.call-done), kind=kOutput, calls=%fused_computation.4 | convolution fusion | flops 1094713344 | bytes 19105792 | tf_op jit(solution)/shard_map/chd,rhd->hcr/dot_general | solution.py:56
  208.9 11.6 %fusion.34 = bf16[512,128]{0,1:T(8,128)(2,1)S(1)} fusion(f32[128,512]{1,0:T(8,128)S(1)} %fusion.20, f32[512,8192]{0,1:T(8,128)} %bitcast_select_fusion, bf16[512,128]{1,0:T(8,128)(2,1)S(1)} %copy-done.5, f32[8192]{0:T(1024)S(1)} %bitcast.286, bf16[2,16384,1,128]{1,3,2,0:T(8,128)(2,1)} %all-gather.5.cloned.1.call-done), kind=kOutput, calls=%fused_computation.54 | convolution fusion | flops 2164391936 | bytes 21528576 | tf_op jit(solution)/shard_map/hcr,rhd->chd/dot_general | solution.py:67
  221.0 8.4 %fusion.16 = f32[128,512]{1,0:T(8,128)} fusion(f32[512,8192]{0,1:T(8,128)} %bitcast_select_fusion, bf16[2,16384,1,128]{1,3,2,0:T(8,128)(2,1)} %all-gather.5.cloned.1.call-done), kind=kOutput, calls=%fused_computation.27 | convolution fusion | flops 1077936128 | bytes 19136512 | tf_op jit(solution)/shard_map/hcr,rhd->chd/dot_general | solution.py:60
  229.4 8.9 %fusion.22 = bf16[1024,512]{0,1:T(8,128)(2,1)S(1)} fusion(bf16[1024,128]{1,0:T(8,128)(2,1)} %param.24, f32[512,1024]{1,0:T(8,128)} %fusion.33, f32[512,1024]{1,0:T(8,128)S(1)} %fusion.64, f32[128,512]{1,0:T(8,128)} %fusion.16, f32[512,8192]{0,1:T(8,128)} %bitcast_select_fusion.1, bf16[2,16384,1,128]{1,3,2,0:T(8,128)(2,1)} %all-gather.5.cloned.1.call-done), kind=kOutput, calls=%fused_computation.42 | convolution fusion | flops 1213857792 | bytes 24641536 | tf_op jit(solution)/shard_map/dot_general | solution.py:171
  238.9 3.9 %collective-permute-start.7 = (bf16[128,512]{1,0:T(8,128)(2,1)S(1)}, bf16[128,512]{1,0:T(8,128)(2,1)S(1)}, u32[]{:S(2)}, u32[]{:S(2)}) collective-permute-start(bf16[128,512]{1,0:T(8,128)(2,1)S(1)} %get-tuple-element.7), channel_id=1, source_target_pairs={{0,1},{1,2},{2,3},{3,4},{4,5},{5,6},{6,7},{7,0},{8,9},{9,10},{10,1... | collective-permute-start | bytes 393224 | tf_op jit(solution)/shard_map/ppermute | solution.py:13
  242.8 4.2 %collective-permute-start.13 = (bf16[128,512]{1,0:T(8,128)(2,1)S(1)}, bf16[128,512]{1,0:T(8,128)(2,1)S(1)}, u32[]{:S(2)}, u32[]{:S(2)}) collective-permute-start(bf16[128,512]{1,0:T(8,128)(2,1)S(1)} %get-tuple-element.8), channel_id=1, source_target_pairs={{0,7},{1,0},{2,1},{3,2},{4,3},{5,4},{6,5},{7,6},{8,15},{9,8},{10,9... | collective-permute-start | bytes 393224 | tf_op jit(solution)/shard_map/ppermute | solution.py:13
  248.6 3.3 %collective-permute-start.11 = (bf16[128,512]{1,0:T(8,128)(2,1)S(1)}, bf16[128,512]{1,0:T(8,128)(2,1)S(1)}, u32[]{:S(2)}, u32[]{:S(2)}) collective-permute-start(bf16[128,512]{1,0:T(8,128)(2,1)S(1)} %get-tuple-element.10), channel_id=1, source_target_pairs={{0,5},{1,6},{2,7},{3,0},{4,1},{5,2},{6,3},{7,4},{8,13},{9,14},{10,... | collective-permute-start | bytes 393224 | tf_op jit(solution)/shard_map/ppermute | solution.py:13
  251.9 2.9 %collective-permute-start.10 = (bf16[128,512]{1,0:T(8,128)(2,1)S(1)}, bf16[128,512]{1,0:T(8,128)(2,1)S(1)}, u32[]{:S(2)}, u32[]{:S(2)}) collective-permute-start(bf16[128,512]{1,0:T(8,128)(2,1)S(1)} %get-tuple-element.11), channel_id=1, source_target_pairs={{0,4},{1,5},{2,6},{3,7},{4,0},{5,1},{6,2},{7,3},{8,12},{9,13},{10,... | collective-permute-start | bytes 393224 | tf_op jit(solution)/shard_map/ppermute | solution.py:13
  254.8 2.6 collective-permute-done.7
  258.6 2.2 collective-permute-done.13
  260.8 1.6 collective-permute-start.8
  262.4 4.8 %collective-permute-done.11 = bf16[128,512]{1,0:T(8,128)(2,1)S(1)} collective-permute-done((bf16[128,512]{1,0:T(8,128)(2,1)S(1)}, bf16[128,512]{1,0:T(8,128)(2,1)S(1)}, u32[]{:S(2)}, u32[]{:S(2)}) %collective-permute-start.11) | collective-permute-done | bytes 131104 | tf_op jit(solution)/shard_map/ppermute | solution.py:13
  267.2 4.1 %collective-permute-done.9 = bf16[128,512]{1,0:T(8,128)(2,1)S(1)} collective-permute-done((bf16[128,512]{1,0:T(8,128)(2,1)S(1)}, bf16[128,512]{1,0:T(8,128)(2,1)S(1)}, u32[]{:S(2)}, u32[]{:S(2)}) %collective-permute-start.9) | collective-permute-done | bytes 131104 | tf_op jit(solution)/shard_map/ppermute | solution.py:13
  (98 shorter events, 20.9 us)
Async XLA Ops:
  6.5 118.8 %copy-start = (bf16[1024,128]{1,0:T(8,128)(2,1)S(1)}, bf16[1024,128]{1,0:T(8,128)(2,1)}, u32[]{:S(2)}) copy-start(bf16[1024,128]{1,0:T(8,128)(2,1)} %param.22) | copy-start | bytes 786436
  6.5 91.8 %copy-start.3 = (bf16[512,128]{1,0:T(8,128)(2,1)S(1)}, bf16[512,128]{1,0:T(8,128)(2,1)}, u32[]{:S(2)}) copy-start(bf16[512,128]{1,0:T(8,128)(2,1)} %param.13) | copy-start | bytes 393220
  6.5 52.3 %copy-start.10 = (s32[4]{0:T(128)S(1)}, s32[4]{0:T(128)}, u32[]{:S(2)}) copy-start(s32[4]{0:T(128)} %param.21) | copy-start | bytes 52
  6.5 52.4 %copy-start.9 = (s32[4,48]{1,0:T(4,128)S(1)}, s32[4,48]{1,0:T(4,128)}, u32[]{:S(2)}) copy-start(s32[4,48]{1,0:T(4,128)} %param.20) | copy-start | bytes 2308
  6.5 53.6 %copy-start.6 = (s32[16384]{0:T(1024)S(1)}, s32[16384]{0:T(1024)}, u32[]{:S(2)}) copy-start(s32[16384]{0:T(1024)} %param.19) | copy-start | bytes 196612
  6.5 53.7 %copy-start.8 = (f32[1,512]{1,0:T(1,128)S(1)}, f32[1,512]{1,0:T(1,128)}, u32[]{:S(2)}) copy-start(f32[1,512]{1,0:T(1,128)} %param.18) | copy-start | bytes 6148
  6.6 91.8 %all-gather.3.cloned.1.call-start = ((), (), s32[]{:S(2)}) async-start(), calls=%async_computation | async-start | bytes 8650752 | tf_op jit(solution)/shard_map/all_gather | solution.py:125
  8.4 155.6 %all-gather.5.cloned.1.call-start = ((), (), s32[]{:S(2)}) async-start(), calls=%async_computation.1 | async-start | bytes 8650752 | tf_op jit(solution)/shard_map/all_gather | solution.py:126
  8.5 46.0 %collective-permute-start.5 = (bf16[512,128]{1,0:T(8,128)(2,1)}, bf16[512,128]{1,0:T(8,128)(2,1)S(1)}, u32[]{:S(2)}, u32[]{:S(2)}) collective-permute-start(bf16[512,128]{1,0:T(8,128)(2,1)} %param.17), channel_id=1, source_target_pairs={{0,6},{1,7},{2,0},{3,1},{4,2},{5,3},{6,4},{7,5},{8,14},{9,15},{10,... | collective-permute-start | bytes 393224 | tf_op jit(solution)/shard_map/ppermute | solution.py:13
  11.3 43.1 %collective-permute-start.4 = (bf16[512,128]{1,0:T(8,128)(2,1)}, bf16[512,128]{1,0:T(8,128)(2,1)S(1)}, u32[]{:S(2)}, u32[]{:S(2)}) collective-permute-start(bf16[512,128]{1,0:T(8,128)(2,1)} %param.17), channel_id=1, source_target_pairs={{0,5},{1,6},{2,7},{3,0},{4,1},{5,2},{6,3},{7,4},{8,13},{9,14},{10,... | collective-permute-start | bytes 393224 | tf_op jit(solution)/shard_map/ppermute | solution.py:13
  17.8 36.5 %collective-permute-start.3 = (bf16[512,128]{1,0:T(8,128)(2,1)}, bf16[512,128]{1,0:T(8,128)(2,1)S(1)}, u32[]{:S(2)}, u32[]{:S(2)}) collective-permute-start(bf16[512,128]{1,0:T(8,128)(2,1)} %param.17), channel_id=1, source_target_pairs={{0,4},{1,5},{2,6},{3,7},{4,0},{5,1},{6,2},{7,3},{8,12},{9,13},{10,... | collective-permute-start | bytes 393224 | tf_op jit(solution)/shard_map/ppermute | solution.py:13
  20.6 19.3 %collective-permute-start.1 = (bf16[512,128]{1,0:T(8,128)(2,1)}, bf16[512,128]{1,0:T(8,128)(2,1)S(1)}, u32[]{:S(2)}, u32[]{:S(2)}) collective-permute-start(bf16[512,128]{1,0:T(8,128)(2,1)} %param.17), channel_id=1, source_target_pairs={{0,2},{1,3},{2,4},{3,5},{4,6},{5,7},{6,0},{7,1},{8,10},{9,11},{10,... | collective-permute-start | bytes 393224 | tf_op jit(solution)/shard_map/ppermute | solution.py:13
  20.6 15.8 %collective-permute-start = (bf16[512,128]{1,0:T(8,128)(2,1)}, bf16[512,128]{1,0:T(8,128)(2,1)S(1)}, u32[]{:S(2)}, u32[]{:S(2)}) collective-permute-start(bf16[512,128]{1,0:T(8,128)(2,1)} %param.17), channel_id=1, source_target_pairs={{0,1},{1,2},{2,3},{3,4},{4,5},{5,6},{6,7},{7,0},{8,9},{9,10},{10,1... | collective-permute-start | bytes 393224 | tf_op jit(solution)/shard_map/ppermute | solution.py:13
  36.3 18.0 %collective-permute-start.2 = (bf16[512,128]{1,0:T(8,128)(2,1)}, bf16[512,128]{1,0:T(8,128)(2,1)S(1)}, u32[]{:S(2)}, u32[]{:S(2)}) collective-permute-start(bf16[512,128]{1,0:T(8,128)(2,1)} %param.17), channel_id=1, source_target_pairs={{0,3},{1,4},{2,5},{3,6},{4,7},{5,0},{6,1},{7,2},{8,11},{9,12},{10,... | collective-permute-start | bytes 393224 | tf_op jit(solution)/shard_map/ppermute | solution.py:13
  39.8 17.7 %collective-permute-start.6 = (bf16[512,128]{1,0:T(8,128)(2,1)}, bf16[512,128]{1,0:T(8,128)(2,1)S(1)}, u32[]{:S(2)}, u32[]{:S(2)}) collective-permute-start(bf16[512,128]{1,0:T(8,128)(2,1)} %param.17), channel_id=1, source_target_pairs={{0,7},{1,0},{2,1},{3,2},{4,3},{5,4},{6,5},{7,6},{8,15},{9,8},{10,9... | collective-permute-start | bytes 393224 | tf_op jit(solution)/shard_map/ppermute | solution.py:13
  98.4 3.7 %copy-start.2 = (bf16[2,16384,1,128]{3,1,2,0:T(8,128)(2,1)S(1)}, bf16[2,16384,1,128]{3,1,2,0:T(8,128)(2,1)}, u32[]{:S(2)}) copy-start(bf16[2,16384,1,128]{3,1,2,0:T(8,128)(2,1)} %all-gather.3.cloned.1.call-done) | copy-start | bytes 25165828
  123.8 40.3 %copy-start.4 = (bf16[512,128]{1,0:T(8,128)(2,1)S(1)}, bf16[512,128]{1,0:T(8,128)(2,1)}, u32[]{:S(2)}) copy-start(bf16[512,128]{1,0:T(8,128)(2,1)} %param.14) | copy-start | bytes 393220
  164.1 23.2 %copy-start.5 = (bf16[512,128]{1,0:T(8,128)(2,1)S(1)}, bf16[512,128]{1,0:T(8,128)(2,1)}, u32[]{:S(2)}) copy-start(bf16[512,128]{1,0:T(8,128)(2,1)} %param.15) | copy-start | bytes 393220
  208.9 11.7 %copy-start.7 = (bf16[1024,128]{1,0:T(8,128)(2,1)S(1)}, bf16[1024,128]{1,0:T(8,128)(2,1)}, u32[]{:S(2)}) copy-start(bf16[1024,128]{1,0:T(8,128)(2,1)} %param.23) | copy-start | bytes 786436
  229.4 42.8 %copy-start.1 = (bf16[1024,128]{1,0:T(8,128)(2,1)S(1)}, bf16[1024,128]{1,0:T(8,128)(2,1)}, u32[]{:S(2)}) copy-start(bf16[1024,128]{1,0:T(8,128)(2,1)} %param.22) | copy-start | bytes 786436
  238.9 18.5 %collective-permute-start.7 = (bf16[128,512]{1,0:T(8,128)(2,1)S(1)}, bf16[128,512]{1,0:T(8,128)(2,1)S(1)}, u32[]{:S(2)}, u32[]{:S(2)}) collective-permute-start(bf16[128,512]{1,0:T(8,128)(2,1)S(1)} %get-tuple-element.7), channel_id=1, source_target_pairs={{0,1},{1,2},{2,3},{3,4},{4,5},{5,6},{6,7},{7,0},{8,9},{9,10},{10,1... | collective-permute-start | bytes 393224 | tf_op jit(solution)/shard_map/ppermute | solution.py:13
  242.8 18.0 %collective-permute-start.13 = (bf16[128,512]{1,0:T(8,128)(2,1)S(1)}, bf16[128,512]{1,0:T(8,128)(2,1)S(1)}, u32[]{:S(2)}, u32[]{:S(2)}) collective-permute-start(bf16[128,512]{1,0:T(8,128)(2,1)S(1)} %get-tuple-element.8), channel_id=1, source_target_pairs={{0,7},{1,0},{2,1},{3,2},{4,3},{5,4},{6,5},{7,6},{8,15},{9,8},{10,9... | collective-permute-start | bytes 393224 | tf_op jit(solution)/shard_map/ppermute | solution.py:13
  247.0 15.3 %collective-permute-start.12 = (bf16[128,512]{1,0:T(8,128)(2,1)S(1)}, bf16[128,512]{1,0:T(8,128)(2,1)S(1)}, u32[]{:S(2)}, u32[]{:S(2)}) collective-permute-start(bf16[128,512]{1,0:T(8,128)(2,1)S(1)} %get-tuple-element.9), channel_id=1, source_target_pairs={{0,6},{1,7},{2,0},{3,1},{4,2},{5,3},{6,4},{7,5},{8,14},{9,15},{10,... | collective-permute-start | bytes 393224 | tf_op jit(solution)/shard_map/ppermute | solution.py:13
  248.6 18.6 %collective-permute-start.11 = (bf16[128,512]{1,0:T(8,128)(2,1)S(1)}, bf16[128,512]{1,0:T(8,128)(2,1)S(1)}, u32[]{:S(2)}, u32[]{:S(2)}) collective-permute-start(bf16[128,512]{1,0:T(8,128)(2,1)S(1)} %get-tuple-element.10), channel_id=1, source_target_pairs={{0,5},{1,6},{2,7},{3,0},{4,1},{5,2},{6,3},{7,4},{8,13},{9,14},{10,... | collective-permute-start | bytes 393224 | tf_op jit(solution)/shard_map/ppermute | solution.py:13
  251.9 15.3 %collective-permute-start.10 = (bf16[128,512]{1,0:T(8,128)(2,1)S(1)}, bf16[128,512]{1,0:T(8,128)(2,1)S(1)}, u32[]{:S(2)}, u32[]{:S(2)}) collective-permute-start(bf16[128,512]{1,0:T(8,128)(2,1)S(1)} %get-tuple-element.11), channel_id=1, source_target_pairs={{0,4},{1,5},{2,6},{3,7},{4,0},{5,1},{6,2},{7,3},{8,12},{9,13},{10,... | collective-permute-start | bytes 393224 | tf_op jit(solution)/shard_map/ppermute | solution.py:13
  257.4 13.9 %collective-permute-start.9 = (bf16[128,512]{1,0:T(8,128)(2,1)S(1)}, bf16[128,512]{1,0:T(8,128)(2,1)S(1)}, u32[]{:S(2)}, u32[]{:S(2)}) collective-permute-start(bf16[128,512]{1,0:T(8,128)(2,1)S(1)} %get-tuple-element.12), channel_id=1, source_target_pairs={{0,3},{1,4},{2,5},{3,6},{4,7},{5,0},{6,1},{7,2},{8,11},{9,12},{10,... | collective-permute-start | bytes 393224 | tf_op jit(solution)/shard_map/ppermute | solution.py:13
  260.8 10.5 %collective-permute-start.8 = (bf16[128,512]{1,0:T(8,128)(2,1)S(1)}, bf16[128,512]{1,0:T(8,128)(2,1)S(1)}, u32[]{:S(2)}, u32[]{:S(2)}) collective-permute-start(bf16[128,512]{1,0:T(8,128)(2,1)S(1)} %get-tuple-element.13), channel_id=1, source_target_pairs={{0,2},{1,3},{2,4},{3,5},{4,6},{5,7},{6,0},{7,1},{8,10},{9,11},{10,... | collective-permute-start | bytes 393224 | tf_op jit(solution)/shard_map/ppermute | solution.py:13
Sparse Core Ops, SparseCore 0:
  9.2 84.4 all-gather.2
  95.6 68.3 all-gather.4
where the time goes:
time: 280 us; the launch traced here: 279 us
  matrix products  106 us (38%)
  waiting for transfers between devices  71.7 us (26%)
  starting transfers between devices  37.6 us (13%)
  blocking collectives  37.2 us (13%)
  between operations  14.2 us (5%)
  local copies, waits for them, and re-layouts  9.62 us (3%)
  other arithmetic  3.24 us (1%)
    ppermute x14, waiting for transfers between devices, from_behind(): lax.ppermute(value, axis, [(i, (i + by) % count) for i in range(count)])  38.1 us
    ppermute x14, starting transfers between devices, from_behind(): lax.ppermute(value, axis, [(i, (i + by) % count) for i in range(count)])  37.5 us
    all_gather x1, blocking collectives, per_device(): stats_all = lax.all_gather(stats, 'seq', axis=1, tiled=True)  37.2 us
    all_gather x1, waiting for transfers between devices, per_device(): lax.all_gather(jnp.stack([query_heads, grad_heads]), 'seq', axis=1, tiled...  33.6 us
    dot_general x2, matrix products, key_grads(): jnp.einsum('chd,rhd->hcr', key_heads, query_heads, preferred_element_type...  33.2 us
    dot_general x2, matrix products, key_grads(): jnp.einsum('hcr,rhd->chd', score_grad, query_heads, preferred_element_typ...  23.2 us
    dot_general x4, matrix products, query_grads(): jnp.einsum('rhd,chd->hrc', grad_heads, value_heads, preferred_element_typ...  17.2 us
    dot_general x1, matrix products, per_device(): lax.dot_general(w_value, d_value, contract, preferred_element_type=jnp.fl...  8.85 us
  transfers between devices with their start and end apart: 16, of which 8 were waited for; matrix products, arithmetic and copies ran while one was open for 14% of the time, Pallas kernels for 0%

commit v1 on v0

--- a/solution.py
+++ b/solution.py
@@ -134,7 +134,7 @@
     delta_all = stats_all[heads_here:2 * heads_here]
     allowed_all = stats_all[2 * heads_here:].reshape(seq_count, tiles_here, -1)
     allowed_all = allowed_all.reshape(seq_count * tiles_here, -1)[:, : seq_count * tiles_here] > 0.5
-    chunk = min(total_tokens, 4096)
+    chunk = min(total_tokens, 8192)
     query_sum = None
     for first in range(0, total_tokens, chunk):
         listed = allowed[:, first // TILE:(first + chunk) // TILE]

time: 280 us -> 278 us (level); the launches traced: 279 us -> 273 us
  waiting for transfers between devices: 71.7 us -> 58.2 us
  matrix products: 106 us -> 111 us
  starting transfers between devices: 37.6 us -> 41 us
    ppermute x14, waiting for transfers between devices: 38.1 us -> 25.5 us  [from_behind(): lax.ppermute(value, axis, [(i, (i + by) % count) for i in range(count)])]
    dot_general x2, matrix products: 33.2 us -> 29.3 us  [key_grads(): jnp.einsum('chd,rhd->hcr', key_heads, query_heads, preferred_element_type...]
    all_gather x1, waiting for transfers between devices: 33.6 us -> 30.1 us  [per_device(): lax.all_gather(jnp.stack([query_heads, grad_heads]), 'seq', axis=1, tiled...]
    ppermute x14, starting transfers between devices: 37.5 us -> 40.9 us  [from_behind(): lax.ppermute(value, axis, [(i, (i + by) % count) for i in range(count)])]
    dot_general x3 -> x1, matrix products: 2.24 us -> 5.47 us  [query_grads(): jnp.einsum('hrc,chd->rhd', score_grad, key_heads, preferred_element_type=...]
    dot_general x4 -> x2, matrix products: 17.2 us -> 20 us  [query_grads(): jnp.einsum('rhd,chd->hrc', grad_heads, value_heads, preferred_element_typ...]
    dot_general x4 -> x2, matrix products: 6.39 us -> 7.86 us  [query_grads(): jnp.einsum('rhd,chd->hrc', query_heads, key_heads, preferred_element_type...]
  transfers between devices with their start and end apart: 16 -> 16, of which waited for: 8 -> 7; matrix products, arithmetic and copies ran while one was open for 14% -> 18% of each run, Pallas kernels for 0% -> 0%
where the time goes in v1:
time: 278 us; the launch traced here: 273 us
  matrix products  111 us (40%)
  waiting for transfers between devices  58.2 us (21%)
  starting transfers between devices  41 us (15%)
  blocking collectives  37 us (13%)
  between operations  14.1 us (5%)
  local copies, waits for them, and re-layouts  8.17 us (3%)
  other arithmetic  3.23 us (1%)
    ppermute x14, starting transfers between devices, from_behind(): lax.ppermute(value, axis, [(i, (i + by) % count) for i in range(count)])  40.9 us
    all_gather x1, blocking collectives, per_device(): stats_all = lax.all_gather(stats, 'seq', axis=1, tiled=True)  37 us
    all_gather x1, waiting for transfers between devices, per_device(): lax.all_gather(jnp.stack([query_heads, grad_heads]), 'seq', axis=1, tiled...  30.1 us
    dot_general x2, matrix products, key_grads(): jnp.einsum('chd,rhd->hcr', key_heads, query_heads, preferred_element_type...  29.3 us
    ppermute x14, waiting for transfers between devices, from_behind(): lax.ppermute(value, axis, [(i, (i + by) % count) for i in range(count)])  25.5 us
    dot_general x2, matrix products, key_grads(): jnp.einsum('hcr,rhd->chd', score_grad, query_heads, preferred_element_typ...  23.3 us
    dot_general x2, matrix products, query_grads(): jnp.einsum('rhd,chd->hrc', grad_heads, value_heads, preferred_element_typ...  20 us
    dot_general x1, matrix products, per_device(): lax.dot_general(w_value, d_value, contract, preferred_element_type=jnp.fl...  8.85 us
  transfers between devices with their start and end apart: 16, of which 7 were waited for; matrix products, arithmetic and copies ran while one was open for 18% of the time, Pallas kernels for 0%

profile of v1, /device:TPU:32, one launch (start us, length us, event | category | flops | bytes accessed | tf_op | source)
XLA Modules:
  0.0 273.1 jit_solution(5839582397352790192)
XLA Ops:
  6.6 1.8 pad_maximum_fusion
  8.5 6.4 %collective-permute-start = (bf16[512,128]{1,0:T(8,128)(2,1)}, bf16[512,128]{1,0:T(8,128)(2,1)S(1)}, u32[]{:S(2)}, u32[]{:S(2)}) collective-permute-start(bf16[512,128]{1,0:T(8,128)(2,1)} %param.17), channel_id=1, source_target_pairs={{0,1},{1,2},{2,3},{3,4},{4,5},{5,6},{6,7},{7,0},{8,9},{9,10},{10,1... | collective-permute-start | bytes 393224 | tf_op jit(solution)/shard_map/ppermute | solution.py:13
  14.8 1.5 collective-permute-start.1
  17.5 2.0 collective-permute-start.3
  19.5 7.9 %collective-permute-start.4 = (bf16[512,128]{1,0:T(8,128)(2,1)}, bf16[512,128]{1,0:T(8,128)(2,1)S(1)}, u32[]{:S(2)}, u32[]{:S(2)}) collective-permute-start(bf16[512,128]{1,0:T(8,128)(2,1)} %param.17), channel_id=1, source_target_pairs={{0,5},{1,6},{2,7},{3,0},{4,1},{5,2},{6,3},{7,4},{8,13},{9,14},{10,... | collective-permute-start | bytes 393224 | tf_op jit(solution)/shard_map/ppermute | solution.py:13
  32.8 1.5 collective-permute-start.5
  35.1 5.2 %collective-permute-done.4 = bf16[512,128]{1,0:T(8,128)(2,1)S(1)} collective-permute-done((bf16[512,128]{1,0:T(8,128)(2,1)}, bf16[512,128]{1,0:T(8,128)(2,1)S(1)}, u32[]{:S(2)}, u32[]{:S(2)}) %collective-permute-start.4) | collective-permute-done | bytes 131104 | tf_op jit(solution)/shard_map/ppermute | solution.py:13
  40.4 8.9 %collective-permute-done.6 = bf16[512,128]{1,0:T(8,128)(2,1)S(1)} collective-permute-done((bf16[512,128]{1,0:T(8,128)(2,1)}, bf16[512,128]{1,0:T(8,128)(2,1)S(1)}, u32[]{:S(2)}, u32[]{:S(2)}) %collective-permute-start.6) | collective-permute-done | bytes 131104 | tf_op jit(solution)/shard_map/ppermute | solution.py:13
  51.6 37.0 %all_gather.11 = f32[3,16384]{1,0:T(4,128)S(1)} all-gather(f32[3,512]{1,0:T(4,128)S(1)} %pad_maximum_fusion.2), channel_id=1, replica_groups=mesh['seq'=32,'head'=8] {'seq'}, dimensions={1}, use_global_device_ids=true | all-gather | bytes 202752 | tf_op jit(solution)/shard_map/all_gather | solution.py:131
  89.5 2.5 all-gather.3.cloned.1.call-done
  92.0 3.9 %fusion.17 = f32[8192,512]{1,0:T(8,128)S(1)} fusion(bf16[512,128]{1,0:T(8,128)(2,1)S(1)} %copy-done.2, bf16[2,16384,1,128]{3,1,2,0:T(8,128)(2,1)} %all-gather.3.cloned.1.call-done), kind=kOutput, calls=%fused_computation.37 | convolution fusion | flops 1073741824 | bytes 19005440 | tf_op jit(solution)/shard_map/rhd,chd->hrc/dot_general | solution.py:42
  95.9 10.1 %fusion.9 = bf16[512,8192]{0,1:T(8,128)(2,1)} fusion(f32[8192,512]{1,0:T(8,128)S(1)} %fusion.17, bf16[512,128]{0,1:T(8,128)(2,1)S(1)} %get-tuple-element.23, f32[512]{0:T(512)S(1)} %get-tuple-element.22, f32[512]{0:T(512)S(1)} %bitcast.242, s32[512]{0:T(512)S(1)} %dynamic_slice.34, s32[8192]{0:T(1024)S(1)} %get-tuple-element.19, ...), kind=kOutput, calls=%fused_computation.20 | convolution fusion | flops 1111490560 | bytes 27465728 | tf_op jit(solution)/shard_map/rhd,chd->hrc/dot_general | solution.py:46
  106.1 3.9 %fusion.19 = f32[8192,512]{1,0:T(8,128)S(1)} fusion(bf16[512,128]{1,0:T(8,128)(2,1)S(1)} %copy-done.2, bf16[2,16384,1,128]{3,1,2,0:T(8,128)(2,1)} %all-gather.3.cloned.1.call-done), kind=kOutput, calls=%fused_computation.39 | convolution fusion | flops 1073741824 | bytes 19005440 | tf_op jit(solution)/shard_map/rhd,chd->hrc/dot_general | solution.py:42
  110.0 9.9 %fusion.6 = bf16[512,8192]{0,1:T(8,128)(2,1)} fusion(f32[8192,512]{1,0:T(8,128)S(1)} %fusion.19, bf16[512,128]{0,1:T(8,128)(2,1)S(1)} %get-tuple-element.23, f32[512]{0:T(512)S(1)} %get-tuple-element.22, f32[512]{0:T(512)S(1)} %bitcast.243, s32[512]{0:T(512)S(1)} %dynamic_slice.34, s32[8192]{0:T(1024)S(1)} %get-tuple-element.18, ...), kind=kOutput, calls=%fused_computation.16 | convolution fusion | flops 1111490560 | bytes 27465728 | tf_op jit(solution)/shard_map/rhd,chd->hrc/dot_general | solution.py:46
  119.9 5.5 %fusion.16 = f32[128,512]{1,0:T(8,128)S(1)} fusion(bf16[512,8192]{0,1:T(8,128)(2,1)} %fusion.9, bf16[2,16384,1,128]{3,1,2,0:T(8,128)(2,1)} %all-gather.3.cloned.1.call-done), kind=kOutput, calls=%fused_computation.36 | convolution fusion | flops 1073741824 | bytes 10747904 | tf_op jit(solution)/shard_map/hrc,chd->rhd/dot_general | solution.py:50
  125.4 6.0 %fusion.32 = f32[512,1024]{1,0:T(8,128)S(1)} fusion(bf16[1024,128]{1,0:T(8,128)(2,1)S(1)} %copy-done, f32[128,512]{1,0:T(8,128)S(1)} %fusion.16, bf16[512,8192]{0,1:T(8,128)(2,1)} %fusion.6, bf16[2,16384,1,128]{3,1,2,0:T(8,128)(2,1)} %all-gather.3.cloned.1.call-done), kind=kOutput, calls=%fused_computation.49 | convolution fusion | flops 1208090624 | bytes 13107200 | tf_op jit(solution)/shard_map/dot_general | solution.py:169
  131.3 30.1 %all-gather.5.cloned.1.call-done = bf16[2,16384,1,128]{1,3,2,0:T(8,128)(2,1)} async-done(((bf16[2,512,1,128]{1,3,2,0:T(8,128)(2,1)}), bf16[2,16384,1,128]{1,3,2,0:T(8,128)(2,1)}) %all-gather.5.cloned.1.call-update) | async-done | bytes 8388624 | tf_op jit(solution)/shard_map/all_gather | solution.py:126
  161.4 10.1 %bitcast_select_fusion.1 = f32[512,8192]{0,1:T(8,128)} fusion(bf16[512,128]{1,0:T(8,128)(2,1)S(1)} %copy-done.3, f32[8192]{0:T(1024)S(1)} %bitcast.234, s32[512]{0:T(512)S(1)} %dynamic_slice.34, s32[8192]{0:T(1024)S(1)} %get-tuple-element.19, pred[512,64]{0,1:T(8,128)(4,1)S(1)} %bitcast.230, bf16[2,16384,1,128]{1,3,2,0:T(8,128)(2,1)} %all-gather.5.cloned.1.call-done), kind=kOutput, calls=%fused_computation.12 | convolution fusion | flops 1094713344 | bytes 19105792 | tf_op jit(solution)/shard_map/chd,rhd->hcr/dot_general | solution.py:56
  171.5 11.6 %fusion.14 = f32[128,512]{1,0:T(8,128)S(1)} fusion(f32[512,8192]{0,1:T(8,128)} %bitcast_select_fusion.1, bf16[512,128]{1,0:T(8,128)(2,1)S(1)} %copy-done.4, f32[8192]{0:T(1024)S(1)} %bitcast.233, bf16[2,16384,1,128]{1,3,2,0:T(8,128)(2,1)} %all-gather.5.cloned.1.call-done), kind=kOutput, calls=%fused_computation.25 | convolution fusion | flops 2164260864 | bytes 21397504 | tf_op jit(solution)/shard_map/hcr,rhd->chd/dot_general | solution.py:67
  183.1 19.3 %bitcast_select_fusion = f32[512,8192]{0,1:T(8,128)} fusion(bf16[512,128]{1,0:T(8,128)(2,1)S(1)} %copy-done.3, f32[8192]{0:T(1024)S(1)} %bitcast.232, s32[512]{0:T(512)S(1)} %dynamic_slice.34, s32[8192]{0:T(1024)S(1)} %get-tuple-element.18, pred[512,64]{0,1:T(8,128)(4,1)S(1)} %bitcast.229, bf16[2,16384,1,128]{1,3,2,0:T(8,128)(2,1)} %all-gather.5.cloned.1.call-done), kind=kOutput, calls=%fused_computation.8 | convolution fusion | flops 1094713344 | bytes 19105792 | tf_op jit(solution)/shard_map/chd,rhd->hcr/dot_general | solution.py:56
  202.4 11.7 %fusion.33 = bf16[512,128]{0,1:T(8,128)(2,1)S(1)} fusion(f32[128,512]{1,0:T(8,128)S(1)} %fusion.14, f32[512,8192]{0,1:T(8,128)} %bitcast_select_fusion, bf16[512,128]{1,0:T(8,128)(2,1)S(1)} %copy-done.4, f32[8192]{0:T(1024)S(1)} %bitcast.231, bf16[2,16384,1,128]{1,3,2,0:T(8,128)(2,1)} %all-gather.5.cloned.1.call-done), kind=kOutput, calls=%fused_computation.50 | convolution fusion | flops 2164391936 | bytes 21528576 | tf_op jit(solution)/shard_map/hcr,rhd->chd/dot_general | solution.py:67
  214.1 1.8 fusion.57
  215.9 8.4 %fusion.10 = f32[128,512]{1,0:T(8,128)} fusion(f32[512,8192]{0,1:T(8,128)} %bitcast_select_fusion, bf16[2,16384,1,128]{1,3,2,0:T(8,128)(2,1)} %all-gather.5.cloned.1.call-done), kind=kOutput, calls=%fused_computation.21 | convolution fusion | flops 1077936128 | bytes 19136512 | tf_op jit(solution)/shard_map/hcr,rhd->chd/dot_general | solution.py:60
  224.3 8.8 %fusion.20 = bf16[1024,512]{0,1:T(8,128)(2,1)S(1)} fusion(bf16[1024,128]{1,0:T(8,128)(2,1)} %param.24, f32[512,1024]{1,0:T(8,128)S(1)} %fusion.32, f32[512,1024]{1,0:T(8,128)} %fusion.57, f32[128,512]{1,0:T(8,128)} %fusion.10, f32[512,8192]{0,1:T(8,128)} %bitcast_select_fusion.1, bf16[2,16384,1,128]{1,3,2,0:T(8,128)(2,1)} %all-gather.5.cloned.1.call-done), kind=kOutput, calls=%fused_computation.40 | convolution fusion | flops 1213857792 | bytes 24641536 | tf_op jit(solution)/shard_map/dot_general | solution.py:171
  233.8 6.4 %collective-permute-start.13 = (bf16[128,512]{1,0:T(8,128)(2,1)S(1)}, bf16[128,512]{1,0:T(8,128)(2,1)S(1)}, u32[]{:S(2)}, u32[]{:S(2)}) collective-permute-start(bf16[128,512]{1,0:T(8,128)(2,1)S(1)} %get-tuple-element.8), channel_id=1, source_target_pairs={{0,7},{1,0},{2,1},{3,2},{4,3},{5,4},{6,5},{7,6},{8,15},{9,8},{10,9... | collective-permute-start | bytes 393224 | tf_op jit(solution)/shard_map/ppermute | solution.py:13
  240.9 2.2 collective-permute-start.11
  243.1 2.1 collective-permute-start.10
  245.2 2.5 collective-permute-start.9
  247.8 2.0 collective-permute-start.8
  249.7 4.4 %collective-permute-start.7 = (bf16[128,512]{1,0:T(8,128)(2,1)S(1)}, bf16[128,512]{1,0:T(8,128)(2,1)S(1)}, u32[]{:S(2)}, u32[]{:S(2)}) collective-permute-start(bf16[128,512]{1,0:T(8,128)(2,1)S(1)} %get-tuple-element.7), channel_id=1, source_target_pairs={{0,1},{1,2},{2,3},{3,4},{4,5},{5,6},{6,7},{7,0},{8,9},{9,10},{10,1... | collective-permute-start | bytes 393224 | tf_op jit(solution)/shard_map/ppermute | solution.py:13
  254.2 4.6 %collective-permute-done.9 = bf16[128,512]{1,0:T(8,128)(2,1)S(1)} collective-permute-done((bf16[128,512]{1,0:T(8,128)(2,1)S(1)}, bf16[128,512]{1,0:T(8,128)(2,1)S(1)}, u32[]{:S(2)}, u32[]{:S(2)}) %collective-permute-start.9) | collective-permute-done | bytes 131104 | tf_op jit(solution)/shard_map/ppermute | solution.py:13
  258.8 6.3 %collective-permute-done.7 = bf16[128,512]{1,0:T(8,128)(2,1)S(1)} collective-permute-done((bf16[128,512]{1,0:T(8,128)(2,1)S(1)}, bf16[128,512]{1,0:T(8,128)(2,1)S(1)}, u32[]{:S(2)}, u32[]{:S(2)}) %collective-permute-start.7) | collective-permute-done | bytes 131104 | tf_op jit(solution)/shard_map/ppermute | solution.py:13
  (83 shorter events, 12.7 us)
Async XLA Ops:
  6.5 118.8 %copy-start = (bf16[1024,128]{1,0:T(8,128)(2,1)S(1)}, bf16[1024,128]{1,0:T(8,128)(2,1)}, u32[]{:S(2)}) copy-start(bf16[1024,128]{1,0:T(8,128)(2,1)} %param.22) | copy-start | bytes 786436
  6.5 85.4 %copy-start.2 = (bf16[512,128]{1,0:T(8,128)(2,1)S(1)}, bf16[512,128]{1,0:T(8,128)(2,1)}, u32[]{:S(2)}) copy-start(bf16[512,128]{1,0:T(8,128)(2,1)} %param.13) | copy-start | bytes 393220
  6.5 44.1 %copy-start.9 = (s32[4]{0:T(128)S(1)}, s32[4]{0:T(128)}, u32[]{:S(2)}) copy-start(s32[4]{0:T(128)} %param.21) | copy-start | bytes 52
  6.5 44.2 %copy-start.8 = (s32[4,48]{1,0:T(4,128)S(1)}, s32[4,48]{1,0:T(4,128)}, u32[]{:S(2)}) copy-start(s32[4,48]{1,0:T(4,128)} %param.20) | copy-start | bytes 2308
  6.5 45.0 %copy-start.6 = (s32[16384]{0:T(1024)S(1)}, s32[16384]{0:T(1024)}, u32[]{:S(2)}) copy-start(s32[16384]{0:T(1024)} %param.19) | copy-start | bytes 196612
  6.5 45.1 %copy-start.7 = (f32[1,512]{1,0:T(1,128)S(1)}, f32[1,512]{1,0:T(1,128)}, u32[]{:S(2)}) copy-start(f32[1,512]{1,0:T(1,128)} %param.18) | copy-start | bytes 6148
  6.6 85.4 %all-gather.3.cloned.1.call-start = ((), (), s32[]{:S(2)}) async-start(), calls=%async_computation | async-start | bytes 8650752 | tf_op jit(solution)/shard_map/all_gather | solution.py:125
  8.4 153.0 %all-gather.5.cloned.1.call-start = ((), (), s32[]{:S(2)}) async-start(), calls=%async_computation.1 | async-start | bytes 8650752 | tf_op jit(solution)/shard_map/all_gather | solution.py:126
  8.5 24.4 %collective-permute-start = (bf16[512,128]{1,0:T(8,128)(2,1)}, bf16[512,128]{1,0:T(8,128)(2,1)S(1)}, u32[]{:S(2)}, u32[]{:S(2)}) collective-permute-start(bf16[512,128]{1,0:T(8,128)(2,1)} %param.17), channel_id=1, source_target_pairs={{0,1},{1,2},{2,3},{3,4},{4,5},{5,6},{6,7},{7,0},{8,9},{9,10},{10,1... | collective-permute-start | bytes 393224 | tf_op jit(solution)/shard_map/ppermute | solution.py:13
  14.8 19.5 %collective-permute-start.1 = (bf16[512,128]{1,0:T(8,128)(2,1)}, bf16[512,128]{1,0:T(8,128)(2,1)S(1)}, u32[]{:S(2)}, u32[]{:S(2)}) collective-permute-start(bf16[512,128]{1,0:T(8,128)(2,1)} %param.17), channel_id=1, source_target_pairs={{0,2},{1,3},{2,4},{3,5},{4,6},{5,7},{6,0},{7,1},{8,10},{9,11},{10,... | collective-permute-start | bytes 393224 | tf_op jit(solution)/shard_map/ppermute | solution.py:13
  16.3 18.7 %collective-permute-start.2 = (bf16[512,128]{1,0:T(8,128)(2,1)}, bf16[512,128]{1,0:T(8,128)(2,1)S(1)}, u32[]{:S(2)}, u32[]{:S(2)}) collective-permute-start(bf16[512,128]{1,0:T(8,128)(2,1)} %param.17), channel_id=1, source_target_pairs={{0,3},{1,4},{2,5},{3,6},{4,7},{5,0},{6,1},{7,2},{8,11},{9,12},{10,... | collective-permute-start | bytes 393224 | tf_op jit(solution)/shard_map/ppermute | solution.py:13
  17.5 17.5 %collective-permute-start.3 = (bf16[512,128]{1,0:T(8,128)(2,1)}, bf16[512,128]{1,0:T(8,128)(2,1)S(1)}, u32[]{:S(2)}, u32[]{:S(2)}) collective-permute-start(bf16[512,128]{1,0:T(8,128)(2,1)} %param.17), channel_id=1, source_target_pairs={{0,4},{1,5},{2,6},{3,7},{4,0},{5,1},{6,2},{7,3},{8,12},{9,13},{10,... | collective-permute-start | bytes 393224 | tf_op jit(solution)/shard_map/ppermute | solution.py:13
  19.5 20.7 %collective-permute-start.4 = (bf16[512,128]{1,0:T(8,128)(2,1)}, bf16[512,128]{1,0:T(8,128)(2,1)S(1)}, u32[]{:S(2)}, u32[]{:S(2)}) collective-permute-start(bf16[512,128]{1,0:T(8,128)(2,1)} %param.17), channel_id=1, source_target_pairs={{0,5},{1,6},{2,7},{3,0},{4,1},{5,2},{6,3},{7,4},{8,13},{9,14},{10,... | collective-permute-start | bytes 393224 | tf_op jit(solution)/shard_map/ppermute | solution.py:13
  32.8 7.5 %collective-permute-start.5 = (bf16[512,128]{1,0:T(8,128)(2,1)}, bf16[512,128]{1,0:T(8,128)(2,1)S(1)}, u32[]{:S(2)}, u32[]{:S(2)}) collective-permute-start(bf16[512,128]{1,0:T(8,128)(2,1)} %param.17), channel_id=1, source_target_pairs={{0,6},{1,7},{2,0},{3,1},{4,2},{5,3},{6,4},{7,5},{8,14},{9,15},{10,... | collective-permute-start | bytes 393224 | tf_op jit(solution)/shard_map/ppermute | solution.py:13
  34.4 14.9 %collective-permute-start.6 = (bf16[512,128]{1,0:T(8,128)(2,1)}, bf16[512,128]{1,0:T(8,128)(2,1)S(1)}, u32[]{:S(2)}, u32[]{:S(2)}) collective-permute-start(bf16[512,128]{1,0:T(8,128)(2,1)} %param.17), channel_id=1, source_target_pairs={{0,7},{1,0},{2,1},{3,2},{4,3},{5,4},{6,5},{7,6},{8,15},{9,8},{10,9... | collective-permute-start | bytes 393224 | tf_op jit(solution)/shard_map/ppermute | solution.py:13
  125.3 36.1 %copy-start.3 = (bf16[512,128]{1,0:T(8,128)(2,1)S(1)}, bf16[512,128]{1,0:T(8,128)(2,1)}, u32[]{:S(2)}) copy-start(bf16[512,128]{1,0:T(8,128)(2,1)} %param.14) | copy-start | bytes 393220
  161.4 10.1 %copy-start.4 = (bf16[512,128]{1,0:T(8,128)(2,1)S(1)}, bf16[512,128]{1,0:T(8,128)(2,1)}, u32[]{:S(2)}) copy-start(bf16[512,128]{1,0:T(8,128)(2,1)} %param.15) | copy-start | bytes 393220
  202.4 11.7 %copy-start.5 = (bf16[1024,128]{1,0:T(8,128)(2,1)S(1)}, bf16[1024,128]{1,0:T(8,128)(2,1)}, u32[]{:S(2)}) copy-start(bf16[1024,128]{1,0:T(8,128)(2,1)} %param.23) | copy-start | bytes 786436
  224.3 41.8 %copy-start.1 = (bf16[1024,128]{1,0:T(8,128)(2,1)S(1)}, bf16[1024,128]{1,0:T(8,128)(2,1)}, u32[]{:S(2)}) copy-start(bf16[1024,128]{1,0:T(8,128)(2,1)} %param.22) | copy-start | bytes 786436
  233.8 14.0 %collective-permute-start.13 = (bf16[128,512]{1,0:T(8,128)(2,1)S(1)}, bf16[128,512]{1,0:T(8,128)(2,1)S(1)}, u32[]{:S(2)}, u32[]{:S(2)}) collective-permute-start(bf16[128,512]{1,0:T(8,128)(2,1)S(1)} %get-tuple-element.8), channel_id=1, source_target_pairs={{0,7},{1,0},{2,1},{3,2},{4,3},{5,4},{6,5},{7,6},{8,15},{9,8},{10,9... | collective-permute-start | bytes 393224 | tf_op jit(solution)/shard_map/ppermute | solution.py:13
  240.2 9.5 %collective-permute-start.12 = (bf16[128,512]{1,0:T(8,128)(2,1)S(1)}, bf16[128,512]{1,0:T(8,128)(2,1)S(1)}, u32[]{:S(2)}, u32[]{:S(2)}) collective-permute-start(bf16[128,512]{1,0:T(8,128)(2,1)S(1)} %get-tuple-element.9), channel_id=1, source_target_pairs={{0,6},{1,7},{2,0},{3,1},{4,2},{5,3},{6,4},{7,5},{8,14},{9,15},{10,... | collective-permute-start | bytes 393224 | tf_op jit(solution)/shard_map/ppermute | solution.py:13
  240.9 13.2 %collective-permute-start.11 = (bf16[128,512]{1,0:T(8,128)(2,1)S(1)}, bf16[128,512]{1,0:T(8,128)(2,1)S(1)}, u32[]{:S(2)}, u32[]{:S(2)}) collective-permute-start(bf16[128,512]{1,0:T(8,128)(2,1)S(1)} %get-tuple-element.10), channel_id=1, source_target_pairs={{0,5},{1,6},{2,7},{3,0},{4,1},{5,2},{6,3},{7,4},{8,13},{9,14},{10,... | collective-permute-start | bytes 393224 | tf_op jit(solution)/shard_map/ppermute | solution.py:13
  243.1 11.0 %collective-permute-start.10 = (bf16[128,512]{1,0:T(8,128)(2,1)S(1)}, bf16[128,512]{1,0:T(8,128)(2,1)S(1)}, u32[]{:S(2)}, u32[]{:S(2)}) collective-permute-start(bf16[128,512]{1,0:T(8,128)(2,1)S(1)} %get-tuple-element.11), channel_id=1, source_target_pairs={{0,4},{1,5},{2,6},{3,7},{4,0},{5,1},{6,2},{7,3},{8,12},{9,13},{10,... | collective-permute-start | bytes 393224 | tf_op jit(solution)/shard_map/ppermute | solution.py:13
  245.2 13.5 %collective-permute-start.9 = (bf16[128,512]{1,0:T(8,128)(2,1)S(1)}, bf16[128,512]{1,0:T(8,128)(2,1)S(1)}, u32[]{:S(2)}, u32[]{:S(2)}) collective-permute-start(bf16[128,512]{1,0:T(8,128)(2,1)S(1)} %get-tuple-element.12), channel_id=1, source_target_pairs={{0,3},{1,4},{2,5},{3,6},{4,7},{5,0},{6,1},{7,2},{8,11},{9,12},{10,... | collective-permute-start | bytes 393224 | tf_op jit(solution)/shard_map/ppermute | solution.py:13
  247.8 11.0 %collective-permute-start.8 = (bf16[128,512]{1,0:T(8,128)(2,1)S(1)}, bf16[128,512]{1,0:T(8,128)(2,1)S(1)}, u32[]{:S(2)}, u32[]{:S(2)}) collective-permute-start(bf16[128,512]{1,0:T(8,128)(2,1)S(1)} %get-tuple-element.13), channel_id=1, source_target_pairs={{0,2},{1,3},{2,4},{3,5},{4,6},{5,7},{6,0},{7,1},{8,10},{9,11},{10,... | collective-permute-start | bytes 393224 | tf_op jit(solution)/shard_map/ppermute | solution.py:13
  249.7 15.4 %collective-permute-start.7 = (bf16[128,512]{1,0:T(8,128)(2,1)S(1)}, bf16[128,512]{1,0:T(8,128)(2,1)S(1)}, u32[]{:S(2)}, u32[]{:S(2)}) collective-permute-start(bf16[128,512]{1,0:T(8,128)(2,1)S(1)} %get-tuple-element.7), channel_id=1, source_target_pairs={{0,1},{1,2},{2,3},{3,4},{4,5},{5,6},{6,7},{7,0},{8,9},{9,10},{10,1... | collective-permute-start | bytes 393224 | tf_op jit(solution)/shard_map/ppermute | solution.py:13
Sparse Core Ops, SparseCore 0:
  9.2 82.6 all-gather.2
  93.8 67.5 all-gather.4
